TPU v7x, 32 devices: a whole 2x2x4 slice. The times are simulated.
32 devices in a mesh: groups: 2 (over y), fsdp: 4 (over z), segment: 4 (over x, core).
Axes of the slice: x: 2, y: 2, z: 4, core: 2. Of those that a mesh axis runs over, the one named last changes fastest.
Arguments:
- layer_inputs: bfloat16 [32, 8192], P(('groups', 'fsdp'), 'segment'), parts along dimension 0, may hold values from -6 to 6
- labels: int32 [32], P('groups'), parts along dimension 0, may hold values from 0 to 1
- head_weight: float32 [4096], replicated, may hold values from -5 to 5
- gate_up_store: bfloat16 [1280, 4, 2, 128, 128], P('fsdp', 'segment'), may hold values from -0.125 to 0.125
- down_store: bfloat16 [1280, 4, 128, 128], P('fsdp', 'segment'), may hold values from -0.0625 to 0.0625
- kept_rows: int32 [2, 128, 16], replicated, may hold values from 0 to 31, as said below
- owners: int32 [2, 128, 16], replicated, may hold values from 0 to 3, as said below
- slots: int32 [2, 128, 16], replicated, may hold values from 0 to 319, as said below
Outputs:
- input_grads: bfloat16 [32, 8192], P(('groups', 'fsdp'), 'segment'), parts along dimension 0
- gate_up_grads: bfloat16 [2560, 4, 2, 128, 128], P(('groups', 'fsdp'), 'segment'), parts along dimension 0
- down_grads: bfloat16 [2560, 4, 128, 128], P(('groups', 'fsdp'), 'segment'), parts along dimension 0
There are 2 independent parts, one for each index of `groups`. A program takes and returns all parts, laid end to end along the dimension named above; an argument that names none is the same for every part. Nothing has to cross between parts.
Inputs may be any that keep to these rules, and one draw needn't show every extreme that they name: kept_rows[p, j] holds 16 distinct block rows. `owners`: call (j // 16) mod 4 the reader of hidden block column j. For each segment p and each value of j // 64, one fsdp index stores at most 320 of those kept blocks, and at most 80 of them with one reader; both bounds are reached. Kept blocks with the same segment, the same j // 64 and the same owner have distinct slots.
All inputs are finite; a program needn't handle non-finite values.
Results may differ from a plain program's by a relative error of at most 0.008.
Values may be sent and summed in bfloat16 or wider, within the bound.
No kernel may reach another device: no remote copies, remote signals or barrier semaphores. Data moves between devices by JAX's collectives and lax.ppermute only.
A program may use at most 256 MiB of HBM per device.

v0:
```python
import jax
import jax.numpy as jnp
from jax import lax
from jax.sharding import PartitionSpec as P

PIPE = 2
HI = lax.Precision.HIGHEST


def per_device(
    layer_inputs, labels, head_weight, gate_up_store, down_store, kept_rows, owners, slots
):
    members = lax.axis_size("fsdp")
    places = lax.axis_size("segment")
    sections = places // PIPE
    member = lax.axis_index("fsdp")
    place = lax.axis_index("segment")
    segment = place // sections
    section = place % sections
    is_last = segment == PIPE - 1
    tok_rows, piece_width = layer_inputs.shape
    tokens = tok_rows * members
    width = piece_width * sections
    blk = gate_up_store.shape[-1]
    capacity = gate_up_store.shape[0]
    kept = kept_rows.shape[2]
    sec_cols = kept_rows.shape[1] // sections
    nrow = width // blk
    nblocks = sec_cols * kept
    first_col = section * sec_cols
    sec_rows = lax.dynamic_slice(kept_rows, (segment, first_col, 0), (1, sec_cols, kept))
    sec_owner = lax.dynamic_slice(owners, (segment, first_col, 0), (1, sec_cols, kept))
    sec_slot = lax.dynamic_slice(slots, (segment, first_col, 0), (1, sec_cols, kept))
    sec_rows = sec_rows.reshape(nblocks)
    mine = sec_owner.reshape(nblocks) == member
    block_col = jnp.arange(nblocks, dtype=jnp.int32) // kept
    hits = mine[None, :] & (
        sec_slot.reshape(nblocks)[None, :] == jnp.arange(capacity, dtype=jnp.int32)[:, None]
    )
    valid = jnp.any(hits, axis=1)
    slot_col = jnp.sum(jnp.where(hits, block_col[None, :], 0), axis=1)
    slot_row = jnp.sum(jnp.where(hits, sec_rows[None, :], 0), axis=1)
    col_hot = valid[:, None] & (slot_col[:, None] == jnp.arange(sec_cols, dtype=jnp.int32)[None, :])
    row_hot = valid[:, None] & (slot_row[:, None] == jnp.arange(nrow, dtype=jnp.int32)[None, :])
    col_f = col_hot.astype(jnp.float32)
    col_b = col_hot.astype(jnp.bfloat16)
    row_f = row_hot.astype(jnp.float32)
    row_b = row_hot.astype(jnp.bfloat16)
    w_pair = gate_up_store[:, 0]
    w_down = down_store[:, 0]
    gathered = lax.all_gather(layer_inputs, ("fsdp", "segment"))
    gathered = gathered.reshape(members, places, tok_rows, piece_width)
    x_all = gathered.transpose(0, 2, 1, 3).reshape(tokens, places * piece_width)
    x_mine = lax.dynamic_slice_in_dim(x_all, segment * width, width, axis=1)
    x_last = x_all[:, (PIPE - 1) * width :]
    x_sel = jnp.einsum("cr,trb->ctb", row_b, x_mine.reshape(tokens, nrow, blk))
    x_sel = x_sel.astype(jnp.bfloat16)
    gu_slot = jnp.einsum("cta,cgab->ctgb", x_sel, w_pair, preferred_element_type=jnp.float32)
    gu_part = jnp.einsum("cj,ctgb->gtjb", col_f, gu_slot, precision=HI)
    head_rows = head_weight.reshape(nrow, blk)
    head_sel = jnp.einsum("cr,rd->cd", row_f, head_rows, precision=HI)
    folded = jnp.einsum("chd,cd->ch", w_down.astype(jnp.float32), head_sel, precision=HI)
    f_part = jnp.einsum("cj,ch->jh", col_f, folded, precision=HI)
    packed = jnp.concatenate([gu_part.reshape(2 * tokens, sec_cols, blk), f_part[None]], axis=0)
    packed = lax.psum(packed, "fsdp")
    gate = packed[:tokens]
    up = packed[tokens : 2 * tokens]
    f_sum = packed[2 * tokens]
    sig = jax.nn.sigmoid(gate)
    hidden = (gate * sig * up).astype(jnp.bfloat16)
    branch = jnp.einsum("tjh,jh->t", hidden.astype(jnp.float32), f_sum, precision=HI)
    branch = jnp.where(is_last, branch, 0.0)
    branch = lax.psum(branch, "segment")
    x_term = jnp.einsum("td,d->t", x_last.astype(jnp.float32), head_weight, precision=HI)
    logits = (x_term + branch) * width ** (-0.5)
    dlogit = jax.nn.sigmoid(logits) - labels.astype(jnp.float32)
    dout_last = (dlogit[:, None] * head_weight[None, :]).astype(jnp.bfloat16)

    def gate_grads(dhidden):
        dgate = (dhidden * up * sig * (1.0 + gate * (1.0 - sig))).astype(jnp.bfloat16)
        dup = (dhidden * gate * sig).astype(jnp.bfloat16)
        pair = jnp.stack([dgate, dup], axis=2)
        return jnp.einsum("cj,tjgb->ctgb", col_b, pair).astype(jnp.bfloat16)

    def spread_rows(d_sel):
        spread = jnp.einsum("ctgb,cgab->cta", d_sel, w_pair, preferred_element_type=jnp.float32)
        return jnp.einsum("cr,cta->tra", row_f, spread, precision=HI).reshape(tokens, width)

    d_sel_last = gate_grads(dlogit[:, None, None] * f_sum[None])
    part_last = jnp.where(is_last, spread_rows(d_sel_last), 0.0)
    sum_last = lax.psum(part_last, ("fsdp", "segment"))
    grad_last = (dout_last.astype(jnp.float32) + sum_last).astype(jnp.bfloat16)
    dout_sel = jnp.einsum("cr,trd->ctd", row_b, grad_last.reshape(tokens, nrow, blk))
    dout_sel = dout_sel.astype(jnp.bfloat16)
    dh_slot = jnp.einsum("ctd,chd->cth", dout_sel, w_down, preferred_element_type=jnp.float32)
    dh_part = jnp.einsum("cj,cth->tjh", col_f, dh_slot, precision=HI)
    dhidden_first = lax.psum(dh_part, "fsdp")
    d_sel_first = gate_grads(dhidden_first)
    part_first = jnp.where(is_last, 0.0, spread_rows(d_sel_first))
    sum_first = lax.psum(part_first, ("fsdp", "segment"))
    grad_first = (grad_last.astype(jnp.float32) + sum_first).astype(jnp.bfloat16)
    rows_at = member * tok_rows
    cols_at = section * piece_width
    grads = jnp.where(is_last, grad_last, grad_first)
    input_grads = lax.dynamic_slice(grads, (rows_at, cols_at), (tok_rows, piece_width))
    d_sel = jnp.where(is_last, d_sel_last, d_sel_first)
    cot_sel = jnp.where(
        is_last,
        jnp.einsum("cr,trd->ctd", row_b, dout_last.reshape(tokens, nrow, blk)).astype(jnp.bfloat16),
        dout_sel,
    )
    hid_sel = jnp.einsum("cj,tjh->cth", col_b, hidden).astype(jnp.bfloat16)
    grad_pair = jnp.einsum(
        "cta,ctgb->cgab", x_sel, d_sel, preferred_element_type=jnp.float32
    ).astype(jnp.bfloat16)
    grad_down = jnp.einsum(
        "cth,ctd->chd", hid_sel, cot_sel, preferred_element_type=jnp.float32
    ).astype(jnp.bfloat16)
    zero_bf = jnp.zeros((), jnp.bfloat16)
    grad_pair = jnp.where(valid[:, None, None, None], grad_pair, zero_bf)
    grad_down = jnp.where(valid[:, None, None], grad_down, zero_bf)
    return (input_grads, grad_pair[:, None], grad_down[:, None])


def solution(mesh):
    return jax.shard_map(
        per_device,
        mesh=mesh,
        in_specs=(
            P(("groups", "fsdp"), "segment"),
            P("groups"),
            P(),
            P("fsdp", "segment", None, None, None),
            P("fsdp", "segment", None, None),
            P(),
            P(),
            P(),
        ),
        out_specs=(
            P(("groups", "fsdp"), "segment"),
            P(("groups", "fsdp"), "segment", None, None, None),
            P(("groups", "fsdp"), "segment", None, None),
        ),
        check_vma=False,
    )
```

profile of v0, /device:TPU:1, one launch (start us, length us, event | category | flops | bytes accessed | tf_op | source)
XLA Modules:
  0.0 401.1 jit_solution(11632360739966436155)
XLA Ops:
  7.3 0.8 constant_dynamic-slice_fusion
  8.0 0.1 copy.54
  8.2 0.8 dynamic-slice_compare_fusion
  9.0 0.1 copy.53
  9.1 0.1 eq.62
  9.2 0.1 copy.55
  9.3 23.9 %all-gather.1 = bf16[16,4,2048]{2,1,0:T(4,128)(2,1)S(1)} all-gather(bf16[1,4,2048]{2,1,0:T(4,128)(2,1)} %bitcast.150), channel_id=2, replica_groups=mesh['groups'=2,'fsdp'=4,'segment'=4] {'fsdp','segment'}, dimensions={0}, use_global_device_ids=true | all-gather | bytes 278528 | tf_op jit(solution)/shard_map/all_gather | solution.py:51
  33.2 0.2 copy.52
  33.5 0.2 copy.86
  33.7 0.3 fusion.38
  34.0 0.6 select_reduce_fusion
  34.6 1.0 fusion.94
  35.6 0.6 convolution_bitcast_fusion
  36.2 19.3 %fusion.8 = f32[320,1,128]{2,1,0:T(1,128)S(1)} fusion(f32[320,128,1]{1,2,0:T(1,128)S(1)} %bitcast.141, bf16[320,1,128,128]{3,2,1,0:T(8,128)(2,1)} %param.12), kind=kOutput, calls=%fused_computation.9 | convolution fusion | flops 62914560 | bytes 10813440 | tf_op jit(solution)/shard_map/chd,cd->ch/dot_general | solution.py:62
  55.5 0.2 convolution_bitcast_fusion.1
  55.8 9.1 %fusion.4 = f32[320,16,2,128]{3,1,2,0:T(8,128)S(1)} fusion(bf16[320,1,2,128,128]{4,3,2,1,0:T(8,128)(2,1)} %param.11, bf16[320,16,128,1]{2,0,1,3:T(8,128)(2,1)S(1)} %convolution_bitcast_fusion), kind=kOutput, calls=%fused_computation.4 | convolution fusion | flops 335544320 | bytes 27525120 | tf_op jit(solution)/shard_map/cta,cgab->ctgb/dot_general | solution.py:58
  64.9 5.3 %fusion.31 = f32[2,16,64,128]{3,2,0,1:T(8,128)S(1)} fusion(f32[320,16,2,128]{3,1,2,0:T(8,128)S(1)} %fusion.4, s32[320]{0:T(512)S(1)} %get-tuple-element.15, pred[320]{0:T(512)(128)(4,1)S(1)} %fusion.38), kind=kOutput, calls=%fused_computation.28 | convolution fusion | flops 1006673920 | bytes 6293056 | tf_op jit(solution)/shard_map/cj,ctgb->gtjb/dot_general | solution.py:59
  70.3 1.1 pad_maximum_fusion
  71.4 49.9 %all-reduce.5.cloned.1.call-done = f32[33,64,128]{2,1,0:T(8,128)} async-done(((f32[33,64,128]{2,1,0:T(8,128)}), f32[33,64,128]{2,1,0:T(8,128)}) %all-reduce.5.cloned.1.call-update) | async-done | bytes 1081360 | tf_op jit(solution)/shard_map/psum | solution.py:65
  121.4 0.9 fusion.118
  122.2 1.3 multiply_convert_fusion.2
  123.6 0.5 fusion.50
  124.1 6.0 %psum.36 = f32[16]{0:T(128)S(1)} all-reduce(f32[16]{0:T(128)S(1)} %fusion.50), channel_id=1, replica_groups=mesh['groups'=2,'fsdp'=4,'segment'=4] {'segment'}, use_global_device_ids=true, to_apply=%region_4.5 | all-reduce | flops 16 | bytes 128 | tf_op jit(solution)/shard_map/psum | solution.py:73
  130.1 0.3 fusion.57
  130.3 0.3 fusion.73
  130.7 0.9 fusion.63
  131.6 10.8 %fusion.21 = f32[320,16,128]{2,1,0:T(8,128)S(1)} fusion(bf16[320,1,2,128,128]{4,3,2,1,0:T(8,128)(2,1)} %param.11, bf16[320,16,2,128]{3,0,2,1:T(8,128)(2,1)S(1)} %fusion.63), kind=kOutput, calls=%fused_computation.24 | convolution fusion | flops 335544320 | bytes 26214400 | tf_op jit(solution)/shard_map/ctgb,cgab->cta/dot_general | solution.py:86
  142.3 1.8 fusion.42
  144.1 0.9 copy.136
  145.0 1.6 fusion.81
  146.6 87.7 %all-reduce.7.cloned.1.call-done = f32[16,4096]{1,0:T(8,128)} async-done(((f32[16,4096]{1,0:T(8,128)}), f32[16,4096]{1,0:T(8,128)}) %all-reduce.7.cloned.1.call-update) | async-done | bytes 262160 | tf_op jit(solution)/shard_map/psum | solution.py:91
  234.3 1.0 fusion.126
  235.4 0.5 fusion.114
  236.0 8.7 %fusion.6 = f32[320,16,128]{2,1,0:T(8,128)S(1)} fusion(bf16[320,1,128,128]{3,2,1,0:T(8,128)(2,1)} %param.12, bf16[320,16,128]{2,0,1:T(8,128)(2,1)S(1)} %fusion.114), kind=kOutput, calls=%fused_computation.7 | convolution fusion | flops 167772160 | bytes 14417920 | tf_op jit(solution)/shard_map/ctd,chd->cth/dot_general | solution.py:95
  244.7 2.7 fusion.39
  247.5 0.1 add_convert_fusion
  247.6 2.0 convolution_select_fusion
  249.6 10.0 %select_bitcast_fusion.1 = bf16[320,1,128,128]{3,2,1,0:T(8,128)(2,1)} fusion(pred[320]{0:T(512)(128)(4,1)S(1)} %fusion.38, bf16[320,16,128]{2,0,1:T(8,128)(2,1)S(1)} %convolution_select_fusion, bf16[320,16,128]{2,0,1:T(8,128)(2,1)S(1)} %copy-done.4), kind=kOutput, calls=%fused_computation.11 | convolution fusion | flops 178257920 | bytes 13107520 | tf_op jit(solution)/shard_map/cth,ctd->chd/dot_general | solution.py:116
  259.7 25.1 %all-reduce.9.cloned.1.call-done = f32[16,64,128]{2,1,0:T(8,128)} async-done(((f32[16,64,128]{2,1,0:T(8,128)}), f32[16,64,128]{2,1,0:T(8,128)}) %all-reduce.9.cloned.1.call-update) | async-done | bytes 524304 | tf_op jit(solution)/shard_map/psum | solution.py:97
  284.7 1.6 fusion.69
  286.4 2.4 broadcast_select_fusion
  288.8 10.8 %fusion.26 = f32[320,16,128]{2,1,0:T(8,128)S(1)} fusion(bf16[320,1,2,128,128]{4,3,2,1,0:T(8,128)(2,1)} %param.11, bf16[320,16,2,128]{3,0,2,1:T(8,128)(2,1)S(1)} %get-tuple-element.24), kind=kOutput, calls=%fused_computation.25 | convolution fusion | flops 335544320 | bytes 26214400 | tf_op jit(solution)/shard_map/ctgb,cgab->cta/dot_general | solution.py:86
  299.5 1.8 fusion.45
  301.3 0.9 copy.135
  302.2 16.9 %select_bitcast_fusion = bf16[320,1,2,128,128]{3,4,2,0,1:T(8,128)(2,1)} fusion(pred[320]{0:T(512)(128)(4,1)S(1)} %fusion.38, bf16[320,16,2,128]{3,0,2,1:T(8,128)(2,1)} %get-tuple-element.23, bf16[320,16,128,1]{2,0,1,3:T(8,128)(2,1)S(1)} %copy-done.3), kind=kOutput, calls=%fused_computation.6 | convolution fusion | flops 356515840 | bytes 24904000 | tf_op jit(solution)/shard_map/cta,ctgb->cgab/dot_general | solution.py:113
  319.0 27.9 %copy.71 = bf16[320,1,2,128,128]{4,3,2,1,0:T(8,128)(2,1)} copy(bf16[320,1,2,128,128]{3,4,2,0,1:T(8,128)(2,1)} %select_bitcast_fusion) | data formatting | bytes 41943040
  347.0 45.8 %all-reduce.11.cloned.1.call-done = f32[16,4096]{1,0:T(8,128)} async-done(((f32[16,4096]{1,0:T(8,128)}), f32[16,4096]{1,0:T(8,128)}) %all-reduce.11.cloned.1.call-update) | async-done | bytes 262160 | tf_op jit(solution)/shard_map/psum | solution.py:100
  392.8 1.5 fusion.104
  (31 shorter events, 0.6 us)
Async XLA Ops:
  7.2 114.2 %all-reduce.5.cloned.1.call-start = ((), (), s32[]{:S(2)}) async-start(), calls=%async_computation | async-start | bytes 2162688 | tf_op jit(solution)/shard_map/psum | solution.py:65
  36.2 19.6 %copy-start.2 = (bf16[320,16,128,1]{2,0,1,3:T(8,128)(2,1)}, bf16[320,16,128,1]{2,0,1,3:T(8,128)(2,1)S(1)}, u32[]{:S(2)}) copy-start(bf16[320,16,128,1]{2,0,1,3:T(8,128)(2,1)S(1)} %convolution_bitcast_fusion) | copy-start | bytes 3932164
  70.2 59.8 %copy-start.6 = (f32[4096]{0:T(1024)S(1)}, f32[4096]{0:T(1024)}, u32[]{:S(2)}) copy-start(f32[4096]{0:T(1024)} %param.10) | copy-start | bytes 49156
  70.2 59.8 %copy-start.7 = (s32[16]{0:T(128)S(1)}, s32[16]{0:T(128)}, u32[]{:S(2)}) copy-start(s32[16]{0:T(128)} %param.9) | copy-start | bytes 196
  71.4 163.0 %all-reduce.7.cloned.1.call-start = ((), (), s32[]{:S(2)}) async-start(), calls=%async_computation.1 | async-start | bytes 524288 | tf_op jit(solution)/shard_map/psum | solution.py:91
  121.4 9.0 %copy-start.1 = (f32[33,64,128]{2,1,0:T(8,128)S(1)}, f32[33,64,128]{2,1,0:T(8,128)}, u32[]{:S(2)}) copy-start(f32[33,64,128]{2,1,0:T(8,128)} %all-reduce.5.cloned.1.call-done) | copy-start | bytes 3244036
  145.0 139.8 %all-reduce.9.cloned.1.call-start = ((), (), s32[]{:S(2)}) async-start(), calls=%async_computation.2 | async-start | bytes 1048576 | tf_op jit(solution)/shard_map/psum | solution.py:97
  236.0 8.8 %copy-start = (bf16[320,16,128]{2,0,1:T(8,128)(2,1)}, bf16[320,16,128]{2,0,1:T(8,128)(2,1)S(1)}, u32[]{:S(2)}) copy-start(bf16[320,16,128]{2,0,1:T(8,128)(2,1)S(1)} %fusion.114) | copy-start | bytes 3932164
  244.7 2.8 copy-start.5
  247.5 145.3 %all-reduce.11.cloned.1.call-start = ((), (), s32[]{:S(2)}) async-start(), calls=%async_computation.3 | async-start | bytes 524288 | tf_op jit(solution)/shard_map/psum | solution.py:100
  247.5 2.1 copy-start.4
  299.5 2.7 copy-start.3
Sparse Core Ops, SparseCore 0:
  71.5 49.8 all-reduce.4
  145.1 89.1 all-reduce.6
  247.6 37.0 all-reduce.8
  302.3 90.4 all-reduce.10
where the time goes:
time: 405 us; the launch traced here: 401 us
  waiting for transfers between devices  209 us (52%)
  matrix products  107 us (26%)
  local copies, waits for them, and re-layouts  32.3 us (8%)
  blocking collectives  29.9 us (7%)
  between operations  14.3 us (4%)
  other arithmetic  8.74 us (2%)
    psum x1, waiting for transfers between devices, per_device(): sum_last = lax.psum(part_last, ('fsdp', 'segment'))  87.7 us
    psum x1, waiting for transfers between devices, per_device(): packed = lax.psum(packed, 'fsdp')  49.9 us
    psum x1, waiting for transfers between devices, per_device(): sum_first = lax.psum(part_first, ('fsdp', 'segment'))  45.8 us
    unnamed x23, local copies, waits for them, and re-layouts  29.9 us
    psum x1, waiting for transfers between devices, per_device(): dhidden_first = lax.psum(dh_part, 'fsdp')  25.1 us
    all_gather x1, blocking collectives, per_device(): gathered = lax.all_gather(layer_inputs, ('fsdp', 'segment'))  23.9 us
    dot_general x2, matrix products, spread_rows(): jnp.einsum('ctgb,cgab->cta', d_sel, w_pair, preferred_element_type=jnp.fl...  21.5 us
    dot_general x1, matrix products, per_device(): jnp.einsum('chd,cd->ch', w_down.astype(jnp.float32), head_sel, precision=HI)  19.3 us
  transfers between devices with their start and end apart: 4, of which 4 were waited for; matrix products, arithmetic and copies ran while one was open for 15% of the time, Pallas kernels for 0%

commit v1 on v0

--- a/solution.py
+++ b/solution.py
@@ -88,7 +88,7 @@
 
     d_sel_last = gate_grads(dlogit[:, None, None] * f_sum[None])
     part_last = jnp.where(is_last, spread_rows(d_sel_last), 0.0)
-    sum_last = lax.psum(part_last, ("fsdp", "segment"))
+    sum_last = lax.psum(lax.psum(part_last, "segment"), "fsdp")
     grad_last = (dout_last.astype(jnp.float32) + sum_last).astype(jnp.bfloat16)
     dout_sel = jnp.einsum("cr,trd->ctd", row_b, grad_last.reshape(tokens, nrow, blk))
     dout_sel = dout_sel.astype(jnp.bfloat16)

time: 405 us -> 385 us (0.951)
  waiting for transfers between devices: 209 us -> 189 us
    psum x1 -> x2, waiting for transfers between devices: 87.7 us -> 66.5 us  [per_device(): sum_last = lax.psum(lax.psum(part_last, 'segment'), 'fsdp')]
  transfers between devices with their start and end apart: 4 -> 5, of which waited for: 4 -> 5; matrix products, arithmetic and copies ran while one was open for 15% -> 15% of each run, Pallas kernels for 0% -> 0%
where the time goes in v1:
time: 385 us; the launch traced here: 381 us
  waiting for transfers between devices  189 us (49%)
  matrix products  107 us (28%)
  local copies, waits for them, and re-layouts  32.4 us (8%)
  blocking collectives  29.9 us (8%)
  between operations  14.3 us (4%)
  other arithmetic  8.74 us (2%)
    psum x2, waiting for transfers between devices, per_device(): sum_last = lax.psum(lax.psum(part_last, 'segment'), 'fsdp')  66.5 us
    psum x1, waiting for transfers between devices, per_device(): packed = lax.psum(packed, 'fsdp')  49.9 us
    psum x1, waiting for transfers between devices, per_device(): sum_first = lax.psum(part_first, ('fsdp', 'segment'))  45.8 us
    unnamed x23, local copies, waits for them, and re-layouts  29.9 us
    psum x1, waiting for transfers between devices, per_device(): dhidden_first = lax.psum(dh_part, 'fsdp')  26.4 us
    all_gather x1, blocking collectives, per_device(): gathered = lax.all_gather(layer_inputs, ('fsdp', 'segment'))  23.9 us
    dot_general x2, matrix products, spread_rows(): jnp.einsum('ctgb,cgab->cta', d_sel, w_pair, preferred_element_type=jnp.fl...  21.5 us
    dot_general x1, matrix products, per_device(): jnp.einsum('chd,cd->ch', w_down.astype(jnp.float32), head_sel, precision=HI)  19.3 us
  transfers between devices with their start and end apart: 5, of which 5 were waited for; matrix products, arithmetic and copies ran while one was open for 15% of the time, Pallas kernels for 0%

profile of v1, /device:TPU:1, one launch (start us, length us, event | category | flops | bytes accessed | tf_op | source)
XLA Modules:
  0.0 381.3 jit_solution(11271375254940870465)
XLA Ops:
  7.3 0.8 constant_dynamic-slice_fusion
  8.0 0.1 copy.54
  8.2 0.8 dynamic-slice_compare_fusion
  9.0 0.1 copy.53
  9.1 0.1 eq.62
  9.3 23.9 %all-gather.1 = bf16[16,4,2048]{2,1,0:T(4,128)(2,1)S(1)} all-gather(bf16[1,4,2048]{2,1,0:T(4,128)(2,1)} %bitcast.150), channel_id=2, replica_groups=mesh['groups'=2,'fsdp'=4,'segment'=4] {'fsdp','segment'}, dimensions={0}, use_global_device_ids=true | all-gather | bytes 278528 | tf_op jit(solution)/shard_map/all_gather | solution.py:51
  33.2 0.2 copy.52
  33.5 0.2 copy.86
  33.7 0.3 fusion.38
  34.0 0.6 select_reduce_fusion
  34.6 1.0 fusion.94
  35.6 0.6 convolution_bitcast_fusion
  36.2 19.3 %fusion.8 = f32[320,1,128]{2,1,0:T(1,128)S(1)} fusion(f32[320,128,1]{1,2,0:T(1,128)S(1)} %bitcast.141, bf16[320,1,128,128]{3,2,1,0:T(8,128)(2,1)} %param.12), kind=kOutput, calls=%fused_computation.9 | convolution fusion | flops 62914560 | bytes 10813440 | tf_op jit(solution)/shard_map/chd,cd->ch/dot_general | solution.py:62
  55.5 0.2 convolution_bitcast_fusion.1
  55.8 9.1 %fusion.4 = f32[320,16,2,128]{3,1,2,0:T(8,128)S(1)} fusion(bf16[320,1,2,128,128]{4,3,2,1,0:T(8,128)(2,1)} %param.11, bf16[320,16,128,1]{2,0,1,3:T(8,128)(2,1)S(1)} %convolution_bitcast_fusion), kind=kOutput, calls=%fused_computation.4 | convolution fusion | flops 335544320 | bytes 27525120 | tf_op jit(solution)/shard_map/cta,cgab->ctgb/dot_general | solution.py:58
  64.9 5.3 %fusion.31 = f32[2,16,64,128]{3,2,0,1:T(8,128)S(1)} fusion(f32[320,16,2,128]{3,1,2,0:T(8,128)S(1)} %fusion.4, s32[320]{0:T(512)S(1)} %get-tuple-element.15, pred[320]{0:T(512)(128)(4,1)S(1)} %fusion.38), kind=kOutput, calls=%fused_computation.28 | convolution fusion | flops 1006673920 | bytes 6293056 | tf_op jit(solution)/shard_map/cj,ctgb->gtjb/dot_general | solution.py:59
  70.3 1.1 pad_maximum_fusion
  71.4 49.9 %all-reduce.6.cloned.1.call-done = f32[33,64,128]{2,1,0:T(8,128)} async-done(((f32[33,64,128]{2,1,0:T(8,128)}), f32[33,64,128]{2,1,0:T(8,128)}) %all-reduce.6.cloned.1.call-update) | async-done | bytes 1081360 | tf_op jit(solution)/shard_map/psum | solution.py:65
  121.4 0.9 fusion.118
  122.2 1.3 multiply_convert_fusion.2
  123.6 0.5 fusion.50
  124.1 6.0 %psum.43 = f32[16]{0:T(128)S(1)} all-reduce(f32[16]{0:T(128)S(1)} %fusion.50), channel_id=1, replica_groups=mesh['groups'=2,'fsdp'=4,'segment'=4] {'segment'}, use_global_device_ids=true, to_apply=%region_4.5 | all-reduce | flops 16 | bytes 128 | tf_op jit(solution)/shard_map/psum | solution.py:73
  130.1 0.3 fusion.57
  130.3 0.3 fusion.73
  130.7 0.9 fusion.63
  131.6 10.8 %fusion.21 = f32[320,16,128]{2,1,0:T(8,128)S(1)} fusion(bf16[320,1,2,128,128]{4,3,2,1,0:T(8,128)(2,1)} %param.11, bf16[320,16,2,128]{3,0,2,1:T(8,128)(2,1)S(1)} %fusion.63), kind=kOutput, calls=%fused_computation.24 | convolution fusion | flops 335544320 | bytes 26214400 | tf_op jit(solution)/shard_map/ctgb,cgab->cta/dot_general | solution.py:86
  142.3 1.8 fusion.42
  144.1 0.9 copy.136
  145.0 30.3 %all-reduce.8.cloned.1.call-done = f32[16,4096]{1,0:T(8,128)} async-done(((f32[16,4096]{1,0:T(8,128)}), f32[16,4096]{1,0:T(8,128)}) %all-reduce.8.cloned.1.call-update) | async-done | bytes 262160 | tf_op jit(solution)/shard_map/psum | solution.py:91
  175.4 1.6 fusion.81
  177.0 36.3 %all-reduce.10.cloned.1.call-done = f32[16,4096]{1,0:T(8,128)} async-done(((f32[16,4096]{1,0:T(8,128)}), f32[16,4096]{1,0:T(8,128)}) %all-reduce.10.cloned.1.call-update) | async-done | bytes 262160 | tf_op jit(solution)/shard_map/psum | solution.py:91
  213.2 1.0 fusion.126
  214.3 0.6 fusion.114
  214.9 8.7 %fusion.6 = f32[320,16,128]{2,1,0:T(8,128)S(1)} fusion(bf16[320,1,128,128]{3,2,1,0:T(8,128)(2,1)} %param.12, bf16[320,16,128]{2,0,1:T(8,128)(2,1)S(1)} %fusion.114), kind=kOutput, calls=%fused_computation.7 | convolution fusion | flops 167772160 | bytes 14417920 | tf_op jit(solution)/shard_map/ctd,chd->cth/dot_general | solution.py:95
  223.6 2.7 fusion.39
  226.4 0.1 add_convert_fusion
  226.5 2.0 convolution_select_fusion
  228.5 10.0 %select_bitcast_fusion.1 = bf16[320,1,128,128]{3,2,1,0:T(8,128)(2,1)} fusion(pred[320]{0:T(512)(128)(4,1)S(1)} %fusion.38, bf16[320,16,128]{2,0,1:T(8,128)(2,1)S(1)} %convolution_select_fusion, bf16[320,16,128]{2,0,1:T(8,128)(2,1)S(1)} %copy-done.4), kind=kOutput, calls=%fused_computation.11 | convolution fusion | flops 178257920 | bytes 13107520 | tf_op jit(solution)/shard_map/cth,ctd->chd/dot_general | solution.py:116
  238.6 26.4 %all-reduce.12.cloned.1.call-done = f32[16,64,128]{2,1,0:T(8,128)} async-done(((f32[16,64,128]{2,1,0:T(8,128)}), f32[16,64,128]{2,1,0:T(8,128)}) %all-reduce.12.cloned.1.call-update) | async-done | bytes 524304 | tf_op jit(solution)/shard_map/psum | solution.py:97
  264.9 1.6 fusion.69
  266.6 2.4 broadcast_select_fusion
  269.0 10.8 %fusion.26 = f32[320,16,128]{2,1,0:T(8,128)S(1)} fusion(bf16[320,1,2,128,128]{4,3,2,1,0:T(8,128)(2,1)} %param.11, bf16[320,16,2,128]{3,0,2,1:T(8,128)(2,1)S(1)} %get-tuple-element.24), kind=kOutput, calls=%fused_computation.25 | convolution fusion | flops 335544320 | bytes 26214400 | tf_op jit(solution)/shard_map/ctgb,cgab->cta/dot_general | solution.py:86
  279.7 1.8 fusion.45
  281.5 0.9 copy.135
  282.4 16.9 %select_bitcast_fusion = bf16[320,1,2,128,128]{3,4,2,0,1:T(8,128)(2,1)} fusion(pred[320]{0:T(512)(128)(4,1)S(1)} %fusion.38, bf16[320,16,2,128]{3,0,2,1:T(8,128)(2,1)} %get-tuple-element.23, bf16[320,16,128,1]{2,0,1,3:T(8,128)(2,1)S(1)} %copy-done.3), kind=kOutput, calls=%fused_computation.6 | convolution fusion | flops 356515840 | bytes 24904000 | tf_op jit(solution)/shard_map/cta,ctgb->cgab/dot_general | solution.py:113
  299.3 27.9 %copy.71 = bf16[320,1,2,128,128]{4,3,2,1,0:T(8,128)(2,1)} copy(bf16[320,1,2,128,128]{3,4,2,0,1:T(8,128)(2,1)} %select_bitcast_fusion) | data formatting | bytes 41943040
  327.2 45.8 %all-reduce.14.cloned.1.call-done = f32[16,4096]{1,0:T(8,128)} async-done(((f32[16,4096]{1,0:T(8,128)}), f32[16,4096]{1,0:T(8,128)}) %all-reduce.14.cloned.1.call-update) | async-done | bytes 262160 | tf_op jit(solution)/shard_map/psum | solution.py:100
  373.0 1.5 fusion.104
  (34 shorter events, 0.7 us)
Async XLA Ops:
  7.2 114.2 %all-reduce.6.cloned.1.call-start = ((), (), s32[]{:S(2)}) async-start(), calls=%async_computation | async-start | bytes 2162688 | tf_op jit(solution)/shard_map/psum | solution.py:65
  36.2 19.6 %copy-start.2 = (bf16[320,16,128,1]{2,0,1,3:T(8,128)(2,1)}, bf16[320,16,128,1]{2,0,1,3:T(8,128)(2,1)S(1)}, u32[]{:S(2)}) copy-start(bf16[320,16,128,1]{2,0,1,3:T(8,128)(2,1)S(1)} %convolution_bitcast_fusion) | copy-start | bytes 3932164
  70.2 59.8 %copy-start.6 = (f32[4096]{0:T(1024)S(1)}, f32[4096]{0:T(1024)}, u32[]{:S(2)}) copy-start(f32[4096]{0:T(1024)} %param.10) | copy-start | bytes 49156
  70.2 59.8 %copy-start.7 = (s32[16]{0:T(128)S(1)}, s32[16]{0:T(128)}, u32[]{:S(2)}) copy-start(s32[16]{0:T(128)} %param.9) | copy-start | bytes 196
  71.4 103.9 %all-reduce.8.cloned.1.call-start = ((), (), s32[]{:S(2)}) async-start(), calls=%async_computation.1 | async-start | bytes 524288 | tf_op jit(solution)/shard_map/psum | solution.py:91
  121.4 9.0 %copy-start.1 = (f32[33,64,128]{2,1,0:T(8,128)S(1)}, f32[33,64,128]{2,1,0:T(8,128)}, u32[]{:S(2)}) copy-start(f32[33,64,128]{2,1,0:T(8,128)} %all-reduce.6.cloned.1.call-done) | copy-start | bytes 3244036
  145.0 68.2 %all-reduce.10.cloned.1.call-start = ((), (), s32[]{:S(2)}) async-start(), calls=%async_computation.2 | async-start | bytes 524288 | tf_op jit(solution)/shard_map/psum | solution.py:91
  175.3 89.6 %all-reduce.12.cloned.1.call-start = ((), (), s32[]{:S(2)}) async-start(), calls=%async_computation.3 | async-start | bytes 1048576 | tf_op jit(solution)/shard_map/psum | solution.py:97
  214.9 8.8 %copy-start = (bf16[320,16,128]{2,0,1:T(8,128)(2,1)}, bf16[320,16,128]{2,0,1:T(8,128)(2,1)S(1)}, u32[]{:S(2)}) copy-start(bf16[320,16,128]{2,0,1:T(8,128)(2,1)S(1)} %fusion.114) | copy-start | bytes 3932164
  223.6 2.8 copy-start.5
  226.4 146.6 %all-reduce.14.cloned.1.call-start = ((), (), s32[]{:S(2)}) async-start(), calls=%async_computation.4 | async-start | bytes 524288 | tf_op jit(solution)/shard_map/psum | solution.py:100
  226.4 2.1 copy-start.4
  279.7 2.7 copy-start.3
Sparse Core Ops, SparseCore 0:
  71.5 49.8 all-reduce.5
  145.1 30.1 all-reduce.7
  177.7 35.4 all-reduce.9
  226.5 38.4 all-reduce.11
  282.5 90.4 all-reduce.13
